TPU v7x, 32 devices: a whole 2x2x4 slice. The times are simulated.
32 devices in a mesh: rows: 8 (over z, x), cols: 4 (over y, core).
Axes of the slice: x: 2, y: 2, z: 4, core: 2. Of those that a mesh axis runs over, the one named last changes fastest.
Arguments:
- vectors: bfloat16 [64, 131072], P('cols', 'rows'), may hold values from -110 to 110
- tile_vals: bfloat16 [1536, 256, 256], P('rows'), may hold values from -0.21875 to 0.21875
- tile_row: int32 [8, 192], P('rows'), may hold values from 0 to 63
- tile_src: int32 [8, 192], P('rows'), may hold values from 0 to 191, each once within a row
- send_list: int32 [64, 16], P('rows'), may hold values from 0 to 63
- ritz_matrix: bfloat16 [64, 64], P(None, 'cols'), may hold values from -0.75 to 0.75
Outputs:
- rotated: bfloat16 [64, 131072], P('cols', 'rows')
- gram_matrix: float32 [64, 64], P('cols')
- projected: float32 [64, 64], P('cols')
Inputs may be any that keep to these rules, and one draw needn't show every extreme that they name: Each row of tile_src holds every number once, so that each own or received block is read by exactly one tile.
All inputs are finite; a program needn't handle non-finite values.
Results may differ from a plain program's by a relative error of at most 0.0062.
Values may be sent and summed in bfloat16 or wider, within the bound.
No kernel may reach another device: no remote copies, remote signals or barrier semaphores. Data moves between devices by JAX's collectives and lax.ppermute only.
A program may use at most 128 MiB of HBM per device.

v0:
```python
import jax
import jax.numpy as jnp
from jax import lax
from jax.sharding import PartitionSpec as P


def tile_products(sources, tile_block, row_ids, src_ids, nblocks):
    chosen = jnp.take(sources, src_ids, axis=1)
    products = jnp.einsum("ktc,trc->ktr", chosen, tile_block, preferred_element_type=jnp.float32)
    onehot = (row_ids[None, :] == jnp.arange(nblocks, dtype=jnp.int32)[:, None]).astype(jnp.float32)
    summed = jnp.einsum("bt,ktr->kbr", onehot, products, precision=lax.Precision.HIGHEST)
    return summed.reshape(summed.shape[0], -1)


def apply_operator(vectors, tile_vals, tile_row, tile_src, send_list):
    columns, length = vectors.shape
    tile_side = tile_vals.shape[1]
    nblocks = length // tile_side
    blocked = vectors.reshape(columns, nblocks, tile_side)
    outgoing = jnp.take(blocked, send_list.reshape(-1), axis=1)
    incoming = lax.all_to_all(outgoing, "rows", split_axis=1, concat_axis=1, tiled=True)
    row_ids = tile_row.reshape(-1)
    src_ids = tile_src.reshape(-1)
    sources = jnp.concatenate([blocked, incoming], axis=1)
    return tile_products(sources, tile_vals, row_ids, src_ids, nblocks)


def contract_nodes(left_side, right_side):
    return lax.dot_general(
        left_side, right_side, (((1,), (1,)), ((), ())), preferred_element_type=jnp.float32
    )


def body(vectors, tile_vals, tile_row, tile_src, send_list, ritz_matrix):
    first_pass = apply_operator(vectors, tile_vals, tile_row, tile_src, send_list).astype(
        jnp.bfloat16
    )
    second = apply_operator(first_pass, tile_vals, tile_row, tile_src, send_list)
    filtered = (2.0 * second - vectors.astype(jnp.float32)).astype(jnp.bfloat16)
    total_nodes = vectors.shape[1] * lax.axis_size("rows")
    operated = apply_operator(filtered, tile_vals, tile_row, tile_src, send_list).astype(
        jnp.bfloat16
    )
    portion = lax.all_gather(filtered, "cols", axis=0, tiled=True)
    gram_piece = contract_nodes(filtered, portion)
    proj_piece = contract_nodes(operated, portion)
    turned = lax.dot_general(
        ritz_matrix, portion, (((0,), (0,)), ((), ())), preferred_element_type=jnp.float32
    )
    gram_total, proj_total = lax.psum((gram_piece, proj_piece), "rows")
    gram_matrix = gram_total / total_nodes
    projected = proj_total / total_nodes
    rotated = turned.astype(jnp.bfloat16)
    return (rotated, gram_matrix, projected)


def solution(mesh):
    return jax.shard_map(
        body,
        mesh=mesh,
        in_specs=(
            P("cols", "rows"),
            P("rows", None, None),
            P("rows", None),
            P("rows", None),
            P("rows", None),
            P(None, "cols"),
        ),
        out_specs=(P("cols", "rows"), P("cols", None), P("cols", None)),
        check_vma=False,
    )
```

profile of v0, /device:TPU:0, one launch (start us, length us, event | category | flops | bytes accessed | tf_op | source)
XLA Modules:
  0.0 207.6 jit_solution(13215640300237485455)
XLA Ops:
  7.2 0.8 reshape.40
  8.0 1.1 copy.41
  9.7 1.2 select_bitcast_fusion.2
  10.9 7.4 %all-to-all-start = ((bf16[16,128,256]{2,0,1:T(8,128)(2,1)}), bf16[16,128,256]{2,0,1:T(8,128)(2,1)S(1)}, u32[]{:S(2)}, u32[]{:S(2)}) async-start(bf16[16,128,256]{2,0,1:T(8,128)(2,1)} %select_bitcast_fusion.2), calls=%async_computation | async-start | bytes 2097152 | tf_op jit(solution)/shard_map/all_to_all | solution.py:21
  18.4 25.7 %all-to-all-done = bf16[16,128,256]{2,0,1:T(8,128)(2,1)S(1)} async-done(((bf16[16,128,256]{2,0,1:T(8,128)(2,1)}), bf16[16,128,256]{2,0,1:T(8,128)(2,1)S(1)}, u32[]{:S(2)}, u32[]{:S(2)}) %all-to-all-start) | async-done | bytes 1048608 | tf_op jit(solution)/shard_map/all_to_all | solution.py:21
  44.2 2.0 gather_fusion.1
  46.3 12.0 %convolution_bitcast_fusion.2 = f32[16,192,256]{2,0,1:T(8,128)S(1)} fusion(bf16[192,256,256]{2,1,0:T(8,128)(2,1)} %param.11, bf16[192,16,256]{2,1,0:T(8,128)(2,1)} %gather_fusion.1, pred[192]{0:T(512)(128)(4,1)S(1)} %compare_and_fusion), kind=kOutput, calls=%fused_computation.16 | convolution fusion | flops 403439616 | bytes 29884608 | tf_op jit(solution)/shard_map/ktc,trc->ktr/dot_general | solution.py:9
  58.3 3.2 %fusion.25 = bf16[16,64,256]{2,1,0:T(8,128)(2,1)S(1)} fusion(f32[16,192,256]{2,0,1:T(8,128)S(1)} %convolution_bitcast_fusion.2, s32[192]{0:T(256)S(1)} %bitcast.65), kind=kOutput, calls=%fused_computation.32 | convolution fusion | flops 604254208 | bytes 3670784 | tf_op jit(solution)/shard_map/bt,ktr->kbr/dot_general | solution.py:11
  62.6 29.3 %all_to_all.15 = bf16[16,128,256]{2,0,1:T(8,128)(2,1)S(1)} all-to-all(bf16[16,128,256]{2,0,1:T(8,128)(2,1)S(1)} %select_bitcast_fusion.1), channel_id=1, replica_groups=mesh['rows'=8,'cols'=4] {'rows'}, dimensions={1} | all-to-all | bytes 2097152 | tf_op jit(solution)/shard_map/all_to_all | solution.py:21
  92.1 2.0 gather_fusion.3
  94.1 12.0 %convolution_bitcast_fusion.1 = f32[16,192,256]{2,0,1:T(8,128)S(1)} fusion(bf16[192,256,256]{2,1,0:T(8,128)(2,1)} %param.11, bf16[192,16,256]{2,1,0:T(8,128)(2,1)} %gather_fusion.3, pred[192]{0:T(512)(128)(4,1)S(1)} %compare_and_fusion), kind=kOutput, calls=%fused_computation.15 | convolution fusion | flops 403439616 | bytes 29884608 | tf_op jit(solution)/shard_map/ktc,trc->ktr/dot_general | solution.py:9
  106.1 3.2 %fusion.16 = f32[16,256,64]{1,2,0:T(8,128)S(1)} fusion(f32[16,192,256]{2,0,1:T(8,128)S(1)} %convolution_bitcast_fusion.1, s32[192]{0:T(256)S(1)} %bitcast.66), kind=kOutput, calls=%fused_computation.29 | convolution fusion | flops 604254208 | bytes 4195072 | tf_op jit(solution)/shard_map/bt,ktr->kbr/dot_general | solution.py:11
  110.5 0.6 gather_fusion.4
  111.2 1.2 select_bitcast_fusion
  112.4 4.2 %all-to-all-start.2 = ((bf16[16,128,256]{2,0,1:T(8,128)(2,1)}), bf16[16,128,256]{2,0,1:T(8,128)(2,1)}, u32[]{:S(2)}, u32[]{:S(2)}) async-start(bf16[16,128,256]{2,0,1:T(8,128)(2,1)} %select_bitcast_fusion), calls=%async_computation.2 | async-start | bytes 2097152 | tf_op jit(solution)/shard_map/all_to_all | solution.py:21
  117.4 24.4 %all-to-all-done.2 = bf16[16,128,256]{2,0,1:T(8,128)(2,1)} async-done(((bf16[16,128,256]{2,0,1:T(8,128)(2,1)}), bf16[16,128,256]{2,0,1:T(8,128)(2,1)}, u32[]{:S(2)}, u32[]{:S(2)}) %all-to-all-start.2) | async-done | bytes 1048608 | tf_op jit(solution)/shard_map/all_to_all | solution.py:21
  141.8 1.4 pad_maximum_fusion.2
  143.2 2.0 gather_fusion.5
  145.2 12.0 %convolution_bitcast_fusion = f32[16,192,256]{2,0,1:T(8,128)S(1)} fusion(bf16[192,256,256]{2,1,0:T(8,128)(2,1)} %param.11, bf16[192,16,256]{2,1,0:T(8,128)(2,1)} %gather_fusion.5, pred[192]{0:T(512)(128)(4,1)S(1)} %compare_and_fusion), kind=kOutput, calls=%fused_computation.14 | convolution fusion | flops 403439616 | bytes 29884608 | tf_op jit(solution)/shard_map/ktc,trc->ktr/dot_general | solution.py:9
  157.2 3.2 %fusion.22 = bf16[16,256,64]{1,2,0:T(8,128)(2,1)S(1)} fusion(f32[16,192,256]{2,0,1:T(8,128)S(1)} %convolution_bitcast_fusion, s32[192]{0:T(256)S(1)} %bitcast.67), kind=kOutput, calls=%fused_computation.31 | convolution fusion | flops 604254208 | bytes 3670784 | tf_op jit(solution)/shard_map/bt,ktr->kbr/dot_general | solution.py:11
  160.7 2.5 %fusion.41 = f32[16,64]{1,0:T(8,128)S(1)} fusion(bf16[16,16384]{1,0:T(8,128)(2,1)} %copy-done.2, bf16[64,16384]{1,0:T(8,128)(2,1)} %all-gather.2.cloned.1.call-done), kind=kOutput, calls=%fused_computation.58 | convolution fusion | flops 33554432 | bytes 2625536 | tf_op jit(solution)/shard_map/dot_general | solution.py:29
  163.3 0.7 fusion.42
  163.9 35.0 %all-reduce = (f32[16,64]{1,0:T(8,128)S(1)}, f32[16,64]{1,0:T(8,128)S(1)}) all-reduce(f32[16,64]{1,0:T(8,128)S(1)} %fusion.41, f32[16,64]{1,0:T(8,128)S(1)} %fusion.42), channel_id=1, replica_groups=mesh['rows'=8,'cols'=4] {'rows'}, use_global_device_ids=true, to_apply=%region_0.3 | all-reduce | flops 2048 | bytes 16384 | tf_op jit(solution)/shard_map/psum | solution.py:50
  199.5 1.2 fusion
  (32 shorter events, 5.0 us)
Async XLA Ops:
  7.2 192.4 %copy-start = (bf16[64,16]{0,1:T(8,128)(2,1)S(1)}, bf16[64,16]{0,1:T(8,128)(2,1)}, u32[]{:S(2)}) copy-start(bf16[64,16]{0,1:T(8,128)(2,1)} %param.15) | copy-start | bytes 6148
  10.9 7.4 %copy-start.5 = (s32[1,192]{1,0:T(1,128)S(1)}, s32[1,192]{1,0:T(1,128)}, u32[]{:S(2)}) copy-start(s32[1,192]{1,0:T(1,128)} %param.13) | copy-start | bytes 2308
  10.9 33.2 %all-to-all-start = ((bf16[16,128,256]{2,0,1:T(8,128)(2,1)}), bf16[16,128,256]{2,0,1:T(8,128)(2,1)S(1)}, u32[]{:S(2)}, u32[]{:S(2)}) async-start(bf16[16,128,256]{2,0,1:T(8,128)(2,1)} %select_bitcast_fusion.2), calls=%async_computation | async-start | bytes 2097152 | tf_op jit(solution)/shard_map/all_to_all | solution.py:21
  46.3 12.1 %copy-start.4 = (s32[1,192]{1,0:T(1,128)S(1)}, s32[1,192]{1,0:T(1,128)}, u32[]{:S(2)}) copy-start(s32[1,192]{1,0:T(1,128)} %param.12) | copy-start | bytes 2308
  109.3 1.0 copy-start.3
  110.4 0.8 copy-start.2
  112.4 29.4 %all-to-all-start.2 = ((bf16[16,128,256]{2,0,1:T(8,128)(2,1)}), bf16[16,128,256]{2,0,1:T(8,128)(2,1)}, u32[]{:S(2)}, u32[]{:S(2)}) async-start(bf16[16,128,256]{2,0,1:T(8,128)(2,1)} %select_bitcast_fusion), calls=%async_computation.2 | async-start | bytes 2097152 | tf_op jit(solution)/shard_map/all_to_all | solution.py:21
  116.7 44.0 %all-gather.2.cloned.1.call-start = ((), (), s32[]{:S(2)}) async-start(), calls=%async_computation.3 | async-start | bytes 2621440 | tf_op jit(solution)/shard_map/all_gather | solution.py:44
  160.7 2.6 %copy-start.1 = (bf16[64,16384]{1,0:T(8,128)(2,1)S(1)}, bf16[64,16384]{1,0:T(8,128)(2,1)}, u32[]{:S(2)}) copy-start(bf16[64,16384]{1,0:T(8,128)(2,1)} %all-gather.2.cloned.1.call-done) | copy-start | bytes 6291460
Sparse Core Ops, SparseCore 0:
  119.6 23.8 all-gather.1
where the time goes:
time: 208 us
  blocking collectives  64.2 us (31%)
  waiting for transfers between devices  50.6 us (24%)
  matrix products  50 us (24%)
  between operations  14.2 us (7%)
  starting transfers between devices  11.9 us (6%)
  local copies, waits for them, and re-layouts  11.7 us (6%)
  other arithmetic  4.96 us (2%)
    all_to_all x2, waiting for transfers between devices, apply_operator(): lax.all_to_all(outgoing, 'rows', split_axis=1, concat_axis=1, tiled=True)  50.1 us
    dot_general x3, matrix products, tile_products(): jnp.einsum('ktc,trc->ktr', chosen, tile_block, preferred_element_type=jnp...  36.1 us
    psum x1, blocking collectives, body(): gram_total, proj_total = lax.psum((gram_piece, proj_piece), 'rows')  35 us
    all_to_all x1, blocking collectives, apply_operator(): lax.all_to_all(outgoing, 'rows', split_axis=1, concat_axis=1, tiled=True)  29.3 us
    all_to_all x2, starting transfers between devices, apply_operator(): lax.all_to_all(outgoing, 'rows', split_axis=1, concat_axis=1, tiled=True)  11.6 us
    dot_general x3, matrix products, tile_products(): jnp.einsum('bt,ktr->kbr', onehot, products, precision=lax.Precision.HIGHEST)  9.49 us
    gather x3, local copies, waits for them, and re-layouts, tile_products(): chosen = jnp.take(sources, src_ids, axis=1)  6.1 us
  transfers between devices with their start and end apart: 3, of which 2 were waited for; matrix products, arithmetic and copies ran while one was open for 9% of the time, Pallas kernels for 0%

commit v1 on v0

--- a/solution.py
+++ b/solution.py
@@ -18,7 +18,10 @@
     nblocks = length // tile_side
     blocked = vectors.reshape(columns, nblocks, tile_side)
     outgoing = jnp.take(blocked, send_list.reshape(-1), axis=1)
-    incoming = lax.all_to_all(outgoing, "rows", split_axis=1, concat_axis=1, tiled=True)
+    incoming = jnp.concatenate(
+        lax.all_to_all(jnp.stack(jnp.split(outgoing, lax.axis_size("rows"), axis=1)), "rows", 0, 0),
+        axis=1,
+    )
     row_ids = tile_row.reshape(-1)
     src_ids = tile_src.reshape(-1)
     sources = jnp.concatenate([blocked, incoming], axis=1)

time: 208 us -> 217 us (1.043)
  local copies, waits for them, and re-layouts: 11.7 us -> 23.2 us
    unnamed x14 -> x37, local copies, waits for them, and re-layouts: 1.45 us -> 11.7 us
where the time goes in v1:
time: 217 us
  blocking collectives  64.3 us (30%)
  waiting for transfers between devices  51 us (24%)
  matrix products  50 us (23%)
  local copies, waits for them, and re-layouts  23.2 us (11%)
  between operations  14.3 us (7%)
  starting transfers between devices  11.2 us (5%)
  other arithmetic  2.98 us (1%)
    all_to_all x2, waiting for transfers between devices, apply_operator(): lax.all_to_all(jnp.stack(jnp.split(outgoing, lax.axis_size('rows'), axis=...  50.6 us
    dot_general x3, matrix products, tile_products(): jnp.einsum('ktc,trc->ktr', chosen, tile_block, preferred_element_type=jnp...  36.1 us
    psum x1, blocking collectives, body(): gram_total, proj_total = lax.psum((gram_piece, proj_piece), 'rows')  35.1 us
    all_to_all x1, blocking collectives, apply_operator(): lax.all_to_all(jnp.stack(jnp.split(outgoing, lax.axis_size('rows'), axis=...  29.3 us
    unnamed x37, local copies, waits for them, and re-layouts  11.7 us
    all_to_all x2, starting transfers between devices, apply_operator(): lax.all_to_all(jnp.stack(jnp.split(outgoing, lax.axis_size('rows'), axis=...  10.9 us
    dot_general x3, matrix products, tile_products(): jnp.einsum('bt,ktr->kbr', onehot, products, precision=lax.Precision.HIGHEST)  9.48 us
    gather x3, local copies, waits for them, and re-layouts, tile_products(): chosen = jnp.take(sources, src_ids, axis=1)  6.1 us
  transfers between devices with their start and end apart: 3, of which 2 were waited for; matrix products, arithmetic and copies ran while one was open for 9% of the time, Pallas kernels for 0%

profile of v1, /device:TPU:0, one launch (start us, length us, event | category | flops | bytes accessed | tf_op | source)
XLA Modules:
  0.0 217.0 jit_solution(14044400899951771982)
XLA Ops:
  7.2 0.8 reshape.58
  8.0 1.1 copy.56
  13.2 0.7 fusion.49
  13.9 0.7 fusion.48
  15.2 7.3 %all-to-all-start = ((bf16[8,16,16,256]{3,1,2,0:T(8,128)(2,1)}), bf16[8,16,16,256]{3,1,2,0:T(8,128)(2,1)S(1)}, u32[]{:S(2)}, u32[]{:S(2)}) async-start(bf16[8,16,16,256]{3,1,2,0:T(8,128)(2,1)} %fusion.47), calls=%async_computation | async-start | bytes 2097152 | tf_op jit(solution)/shard_map/all_to_all | solution.py:22
  22.5 25.7 %all-to-all-done = bf16[8,16,16,256]{3,1,2,0:T(8,128)(2,1)S(1)} async-done(((bf16[8,16,16,256]{3,1,2,0:T(8,128)(2,1)}), bf16[8,16,16,256]{3,1,2,0:T(8,128)(2,1)S(1)}, u32[]{:S(2)}, u32[]{:S(2)}) %all-to-all-start) | async-done | bytes 1048608 | tf_op jit(solution)/shard_map/all_to_all | solution.py:22
  48.4 2.0 gather_fusion.1
  50.4 12.0 %convolution_bitcast_fusion.2 = f32[16,192,256]{2,0,1:T(8,128)S(1)} fusion(bf16[192,256,256]{2,1,0:T(8,128)(2,1)} %param.11, bf16[192,16,256]{2,1,0:T(8,128)(2,1)} %gather_fusion.1, pred[192]{0:T(512)(128)(4,1)S(1)} %compare_and_fusion), kind=kOutput, calls=%fused_computation.16 | convolution fusion | flops 403439616 | bytes 29884608 | tf_op jit(solution)/shard_map/ktc,trc->ktr/dot_general | solution.py:9
  62.5 3.2 %fusion.25 = bf16[16,64,256]{2,1,0:T(8,128)(2,1)S(1)} fusion(f32[16,192,256]{2,0,1:T(8,128)S(1)} %convolution_bitcast_fusion.2, s32[192]{0:T(256)S(1)} %bitcast.173), kind=kOutput, calls=%fused_computation.32 | convolution fusion | flops 604254208 | bytes 3670784 | tf_op jit(solution)/shard_map/bt,ktr->kbr/dot_general | solution.py:11
  66.9 29.3 %all_to_all.15 = bf16[8,16,16,256]{3,1,2,0:T(8,128)(2,1)S(1)} all-to-all(bf16[8,16,16,256]{3,1,2,0:T(8,128)(2,1)S(1)} %fusion.39), channel_id=1, replica_groups=mesh['rows'=8,'cols'=4] {'rows'}, dimensions={0} | all-to-all | bytes 2097152 | tf_op jit(solution)/shard_map/all_to_all | solution.py:22
  96.4 2.0 gather_fusion.3
  98.4 12.0 %convolution_bitcast_fusion.1 = f32[16,192,256]{2,0,1:T(8,128)S(1)} fusion(bf16[192,256,256]{2,1,0:T(8,128)(2,1)} %param.11, bf16[192,16,256]{2,1,0:T(8,128)(2,1)} %gather_fusion.3, pred[192]{0:T(512)(128)(4,1)S(1)} %compare_and_fusion), kind=kOutput, calls=%fused_computation.15 | convolution fusion | flops 403439616 | bytes 29884608 | tf_op jit(solution)/shard_map/ktc,trc->ktr/dot_general | solution.py:9
  110.4 3.2 %fusion.16 = f32[16,256,64]{1,2,0:T(8,128)S(1)} fusion(f32[16,192,256]{2,0,1:T(8,128)S(1)} %convolution_bitcast_fusion.1, s32[192]{0:T(256)S(1)} %bitcast.174), kind=kOutput, calls=%fused_computation.29 | convolution fusion | flops 604254208 | bytes 4195072 | tf_op jit(solution)/shard_map/bt,ktr->kbr/dot_general | solution.py:11
  119.0 0.7 fusion.33
  121.0 3.6 %all-to-all-start.2 = ((bf16[8,16,16,256]{3,1,2,0:T(8,128)(2,1)}), bf16[8,16,16,256]{3,1,2,0:T(8,128)(2,1)S(1)}, u32[]{:S(2)}, u32[]{:S(2)}) async-start(bf16[8,16,16,256]{3,1,2,0:T(8,128)(2,1)} %fusion.31), calls=%async_computation.2 | async-start | bytes 2097152 | tf_op jit(solution)/shard_map/all_to_all | solution.py:22
  125.4 24.8 %all-to-all-done.2 = bf16[8,16,16,256]{3,1,2,0:T(8,128)(2,1)S(1)} async-done(((bf16[8,16,16,256]{3,1,2,0:T(8,128)(2,1)}), bf16[8,16,16,256]{3,1,2,0:T(8,128)(2,1)S(1)}, u32[]{:S(2)}, u32[]{:S(2)}) %all-to-all-start.2) | async-done | bytes 1048608 | tf_op jit(solution)/shard_map/all_to_all | solution.py:22
  150.2 1.0 copy-done.3
  151.2 1.4 pad_maximum_fusion.2
  152.5 2.0 gather_fusion.5
  154.6 12.0 %convolution_bitcast_fusion = f32[16,192,256]{2,0,1:T(8,128)S(1)} fusion(bf16[192,256,256]{2,1,0:T(8,128)(2,1)} %param.11, bf16[192,16,256]{2,1,0:T(8,128)(2,1)} %gather_fusion.5, pred[192]{0:T(512)(128)(4,1)S(1)} %compare_and_fusion), kind=kOutput, calls=%fused_computation.14 | convolution fusion | flops 403439616 | bytes 29884608 | tf_op jit(solution)/shard_map/ktc,trc->ktr/dot_general | solution.py:9
  166.6 3.2 %fusion.22 = bf16[16,256,64]{1,2,0:T(8,128)(2,1)S(1)} fusion(f32[16,192,256]{2,0,1:T(8,128)S(1)} %convolution_bitcast_fusion, s32[192]{0:T(256)S(1)} %bitcast.175), kind=kOutput, calls=%fused_computation.31 | convolution fusion | flops 604254208 | bytes 3670784 | tf_op jit(solution)/shard_map/bt,ktr->kbr/dot_general | solution.py:11
  170.1 2.5 %fusion.65 = f32[16,64]{1,0:T(8,128)S(1)} fusion(bf16[16,16384]{1,0:T(8,128)(2,1)} %copy-done.2, bf16[64,16384]{1,0:T(8,128)(2,1)} %all-gather.2.cloned.1.call-done), kind=kOutput, calls=%fused_computation.106 | convolution fusion | flops 33554432 | bytes 2625536 | tf_op jit(solution)/shard_map/dot_general | solution.py:32
  173.3 35.1 %all-reduce = (f32[16,64]{1,0:T(8,128)S(1)}, f32[16,64]{1,0:T(8,128)S(1)}) all-reduce(f32[16,64]{1,0:T(8,128)S(1)} %fusion.65, f32[16,64]{1,0:T(8,128)S(1)} %fusion.66), channel_id=1, replica_groups=mesh['rows'=8,'cols'=4] {'rows'}, use_global_device_ids=true, to_apply=%region_0.3 | all-reduce | flops 2048 | bytes 16384 | tf_op jit(solution)/shard_map/psum | solution.py:53
  209.0 1.2 fusion
  (58 shorter events, 15.3 us)
Async XLA Ops:
  7.2 201.8 %copy-start = (bf16[64,16]{0,1:T(8,128)(2,1)S(1)}, bf16[64,16]{0,1:T(8,128)(2,1)}, u32[]{:S(2)}) copy-start(bf16[64,16]{0,1:T(8,128)(2,1)} %param.15) | copy-start | bytes 6148
  12.6 9.9 %copy-start.6 = (s32[1,192]{1,0:T(1,128)S(1)}, s32[1,192]{1,0:T(1,128)}, u32[]{:S(2)}) copy-start(s32[1,192]{1,0:T(1,128)} %param.13) | copy-start | bytes 2308
  15.2 33.0 %all-to-all-start = ((bf16[8,16,16,256]{3,1,2,0:T(8,128)(2,1)}), bf16[8,16,16,256]{3,1,2,0:T(8,128)(2,1)S(1)}, u32[]{:S(2)}, u32[]{:S(2)}) async-start(bf16[8,16,16,256]{3,1,2,0:T(8,128)(2,1)} %fusion.47), calls=%async_computation | async-start | bytes 2097152 | tf_op jit(solution)/shard_map/all_to_all | solution.py:22
  50.4 12.1 %copy-start.5 = (s32[1,192]{1,0:T(1,128)S(1)}, s32[1,192]{1,0:T(1,128)}, u32[]{:S(2)}) copy-start(s32[1,192]{1,0:T(1,128)} %param.12) | copy-start | bytes 2308
  113.6 1.0 copy-start.4
  114.7 0.8 copy-start.2
  121.0 29.2 %all-to-all-start.2 = ((bf16[8,16,16,256]{3,1,2,0:T(8,128)(2,1)}), bf16[8,16,16,256]{3,1,2,0:T(8,128)(2,1)S(1)}, u32[]{:S(2)}, u32[]{:S(2)}) async-start(bf16[8,16,16,256]{3,1,2,0:T(8,128)(2,1)} %fusion.31), calls=%async_computation.2 | async-start | bytes 2097152 | tf_op jit(solution)/shard_map/all_to_all | solution.py:22
  124.6 45.5 %all-gather.2.cloned.1.call-start = ((), (), s32[]{:S(2)}) async-start(), calls=%async_computation.3 | async-start | bytes 2621440 | tf_op jit(solution)/shard_map/all_gather | solution.py:47
  150.2 1.0 copy-start.3
  170.1 2.6 %copy-start.1 = (bf16[64,16384]{1,0:T(8,128)(2,1)S(1)}, bf16[64,16384]{1,0:T(8,128)(2,1)}, u32[]{:S(2)}) copy-start(bf16[64,16384]{1,0:T(8,128)(2,1)} %all-gather.2.cloned.1.call-done) | copy-start | bytes 6291460
Sparse Core Ops, SparseCore 0:
  127.6 23.9 all-gather.1
